TPU v7x, 32 devices: a whole 2x2x4 slice. The times are simulated.
32 devices in a mesh: group: 4 (over y, x), dom: 8 (over z, core).
Axes of the slice: x: 2, y: 2, z: 4, core: 2. Of those that a mesh axis runs over, the one named last changes fastest.
Arguments:
- pin_feats: bfloat16 [32768, 256], P(('group', 'dom')), may hold values from -6 to 6
- w_self: bfloat16 [256, 256], replicated, may hold values from -0.375 to 0.375
- w_edge: bfloat16 [4, 256, 256], replicated, may hold values from -0.375 to 0.375
- w_head: bfloat16 [256, 1024], replicated, may hold values from -0.375 to 0.375
- w_out: bfloat16 [1024], replicated, may hold values from -0.1875 to 0.1875
- send_rows: int32 [32, 512], P(('group', 'dom')), may hold values from 0 to 1023
- edge_src: int32 [32, 4, 1024], P(('group', 'dom')), may hold values from 0 to 1535
- edge_dst: int32 [32, 4, 1024], P(('group', 'dom')), may hold values from 0 to 1023
- pin_owner: int32 [32768, 1], P(('group', 'dom')), may hold values from 0 to 31; in each aligned block of 1024 rows (0 to 1023, 1024 to 2047, ...) at most 64 rows name the same one
- pin_net: int32 [32768], P(('group', 'dom')), may hold values from 0 to 255
- net_target: float32 [8192], P(('group', 'dom')), may hold values from -6 to 6
Outputs:
- prediction: float32 [8192], P(('group', 'dom'))
- grad_feats: bfloat16 [32768, 256], P(('group', 'dom'))
- grad_self: float32 [256, 256], replicated
- grad_edge: float32 [4, 256, 256], replicated
- grad_head: float32 [256, 1024], replicated
- grad_out: float32 [1024], replicated
Inputs may be any that keep to these rules, and one draw needn't show every extreme that they name: `pin_owner`: among the pins of one device at most 64 name one owner, and in every draw some device sends exactly 64 pins to some owner.
All inputs are finite; a program needn't handle non-finite values.
Results may differ from a plain program's by a relative error of at most 0.0094.
Values may be sent and summed in bfloat16 or wider, within the bound.
No kernel may reach another device: no remote copies, remote signals or barrier semaphores. Data moves between devices by JAX's collectives and lax.ppermute only.
A program may use at most 64 MiB of HBM per device.

v0:
```python
import math

import jax
import jax.numpy as jnp
from jax import lax
from jax.sharding import PartitionSpec as P


def extended(block, sides, width):
    for axis, dim in sides:
        count = lax.axis_size(axis)
        forward = [(i, i + 1) for i in range(count - 1)]
        backward = [(target, source) for source, target in forward]
        low = lax.ppermute(
            lax.slice_in_dim(block, block.shape[dim] - width, None, axis=dim), axis, forward
        )
        high = lax.ppermute(lax.slice_in_dim(block, 0, width, axis=dim), axis, backward)
        block = jnp.concatenate([low, block, high], axis=dim)
    return block


def silu_slope(values):
    sigma_val = jax.nn.sigmoid(values)
    return sigma_val * (1.0 + values * (1.0 - sigma_val))


def on_device(
    pin_feats,
    w_self,
    w_edge,
    w_head,
    w_out,
    send_rows,
    edge_src,
    edge_dst,
    pin_owner,
    pin_net,
    net_target,
):
    pin_count, feat_width = pin_feats.shape
    send_list = send_rows[0]
    halo_span = send_list.shape[0] // 2
    outgoing = pin_feats[send_list]
    padded = extended(outgoing, (("dom", 0),), halo_span)
    node_table = jnp.concatenate([pin_feats, padded[:halo_span], padded[3 * halo_span :]], 0)
    sources = edge_src[0]
    endpoints = edge_dst[0]
    flat_end = endpoints.reshape(-1)
    gathered = node_table[sources]
    message = jnp.einsum("tek,tkd->ted", gathered, w_edge, preferred_element_type=jnp.float32)
    summed = (
        jnp.zeros((pin_count, feat_width), jnp.float32)
        .at[flat_end]
        .add(message.reshape(-1, feat_width))
    )
    degree = jnp.zeros((pin_count,), jnp.float32).at[flat_end].add(1.0)
    inverse = 1.0 / (1.0 + degree)
    preact = (
        jnp.dot(pin_feats, w_self, preferred_element_type=jnp.float32) + summed * inverse[:, None]
    )
    hidden = jax.nn.silu(preact).astype(jnp.bfloat16)
    groups = lax.axis_size("group")
    domains = lax.axis_size("dom")
    owners = groups * domains
    capacity = max(2, 2 * pin_count // owners)
    net_count = net_target.shape[0]
    owner_ids = pin_owner[:, 0]
    pin_order = jnp.argsort(owner_ids, stable=True)
    sorted_owner = owner_ids[pin_order]
    owner_load = jnp.sum(
        (owner_ids[:, None] == jnp.arange(owners, dtype=jnp.int32)[None, :]).astype(jnp.int32), 0
    )
    load_start = jnp.cumsum(owner_load) - owner_load
    slot_rank = jnp.arange(pin_count, dtype=jnp.int32) - load_start[sorted_owner]
    pin_slot = (
        jnp.zeros((pin_count,), jnp.int32).at[pin_order].set(sorted_owner * capacity + slot_rank)
    )
    outbound = jnp.zeros((owners * capacity, feat_width), jnp.bfloat16).at[pin_slot].set(hidden)
    slot_nets = jnp.full((owners * capacity,), net_count, jnp.int32).at[pin_slot].set(pin_net)
    inbound, slot_nets_in = (
        lax.all_to_all(
            outbound.reshape(owners, capacity, feat_width),
            ("group", "dom"),
            split_axis=0,
            concat_axis=0,
            tiled=True,
        ),
        lax.all_to_all(
            slot_nets.reshape(owners, capacity),
            ("group", "dom"),
            split_axis=0,
            concat_axis=0,
            tiled=True,
        ),
    )
    inbound = inbound.reshape(-1, feat_width)
    slot_nets_in = slot_nets_in.reshape(-1)
    pooled = (
        jnp.zeros((net_count, feat_width), jnp.float32)
        .at[slot_nets_in]
        .add(inbound.astype(jnp.float32), mode="drop")
    )
    pooled_b = pooled.astype(jnp.bfloat16)
    head_pre = jnp.dot(pooled_b, w_head, preferred_element_type=jnp.float32)
    activated = jax.nn.silu(head_pre).astype(jnp.bfloat16)
    predicted = jnp.dot(activated, w_out, preferred_element_type=jnp.float32)
    misfit = predicted - net_target
    head_grad = (
        misfit[:, None] * w_out.astype(jnp.float32)[None, :] * silu_slope(head_pre)
    ).astype(jnp.bfloat16)
    head_sum = jnp.einsum("nd,nh->dh", pooled_b, head_grad, preferred_element_type=jnp.float32)
    out_sum = jnp.dot(misfit, activated.astype(jnp.float32), precision=lax.Precision.HIGHEST)
    net_grad = jnp.einsum(
        "nh,dh->nd", head_grad, w_head, preferred_element_type=jnp.float32
    ).astype(jnp.bfloat16)
    returned = jnp.take(net_grad, slot_nets_in, axis=0, mode="fill", fill_value=0)
    arrived = lax.all_to_all(
        returned.reshape(owners, capacity, feat_width),
        ("group", "dom"),
        split_axis=0,
        concat_axis=0,
        tiled=True,
    )
    pin_grad = arrived.reshape(-1, feat_width)[pin_slot]
    preact_grad = (pin_grad.astype(jnp.float32) * silu_slope(preact)).astype(jnp.bfloat16)
    self_sum = jnp.einsum("pk,pd->kd", pin_feats, preact_grad, preferred_element_type=jnp.float32)
    agg_grad = (preact_grad.astype(jnp.float32) * inverse[:, None]).astype(jnp.bfloat16)
    edge_rows = agg_grad[endpoints]
    edge_sum = jnp.einsum("tek,ted->tkd", gathered, edge_rows, preferred_element_type=jnp.float32)
    gathered_grad = jnp.einsum(
        "ted,tkd->tek", edge_rows, w_edge, preferred_element_type=jnp.float32
    )
    table_grad = (
        jnp.zeros((node_table.shape[0], feat_width), jnp.float32)
        .at[sources.reshape(-1)]
        .add(gathered_grad.reshape(-1, feat_width))
    )
    local_grad = (
        jnp.einsum("pd,kd->pk", preact_grad, w_self, preferred_element_type=jnp.float32)
        + table_grad[:pin_count]
    )
    halo_grad = table_grad[pin_count:].astype(jnp.bfloat16)
    back_padded = extended(halo_grad, (("dom", 0),), halo_span)
    received = jnp.concatenate([back_padded[:halo_span], back_padded[3 * halo_span :]], 0)
    grad_feats = local_grad.at[send_list].add(received.astype(jnp.float32)).astype(jnp.bfloat16)
    totals = lax.psum((self_sum, edge_sum, head_sum, out_sum), ("group", "dom"))
    grad_scale = 1.0 / math.sqrt(pin_count * owners)
    return (
        predicted,
        grad_feats,
        totals[0] * grad_scale,
        totals[1] * grad_scale,
        totals[2] * grad_scale,
        totals[3] * grad_scale,
    )


def solution(mesh):
    in_specs = (
        P(("group", "dom"), None),
        P(),
        P(),
        P(),
        P(),
        P(("group", "dom"), None),
        P(("group", "dom"), None, None),
        P(("group", "dom"), None, None),
        P(("group", "dom"), None),
        P(("group", "dom")),
        P(("group", "dom")),
    )
    out_specs = (P(("group", "dom")), P(("group", "dom"), None), P(), P(), P(), P())
    return jax.shard_map(
        on_device, mesh=mesh, in_specs=in_specs, out_specs=out_specs, check_vma=False
    )
```

profile of v0, /device:TPU:1, one launch (start us, length us, event | category | flops | bytes accessed | tf_op | source)
XLA Modules:
  0.0 407.9 jit_solution(63829753475111449)
XLA Ops:
  7.2 0.9 convert_reduce_fusion
  8.2 0.1 reduce.1
  8.3 0.7 fusion.31
  9.1 0.7 fusion.30
  9.8 5.1 %sort.17 = (s32[1024]{0:T(1024)}, s32[1024]{0:T(1024)S(1)}) sort(s32[1024]{0:T(1024)} %bitcast.101, s32[1024]{0:T(1024)S(1)} %iota.11), dimensions={0}, to_apply=%region_0.0 | sort | flops 10240 | bytes 16384 | tf_op jit(solution)/shard_map/jit(argsort)/sort | solution.py:68
  14.9 4.5 %gather_fusion = s32[1024]{0:T(1024)S(1)} fusion(s32[1024]{0:T(1024)S(1)} %bitcast.102, s32[1024]{0:T(1024)S(1)} %get-tuple-element.70), kind=kCustom, calls=%fused_computation | custom fusion | bytes 12288 | tf_op jit(solution)/shard_map/gather | solution.py:69
  19.4 4.4 %compare_select_fusion.7 = (s32[1024,1]{0,1:T(1,128)S(1)}, s32[1024,1]{0,1:T(1,128)S(1)}) fusion(s32[]{:T(128)} %bitcast.28, s32[]{:T(128)} %bitcast.29, s32[]{:T(128)} %bitcast.30, s32[]{:T(128)} %bitcast.31, s32[]{:T(128)} %bitcast.32, s32[]{:T(128)} %bitcast.34, s32[]{:T(128)} %bitcast.33, s32[1024,1]{0,1:T(1,128)S(1)} %bitcast.118), kind=kLoop, calls=%fused_computation.87 | loop fusion | flops 15360 | bytes 12316 | tf_op jit(solution)/shard_map/gather | solution.py:74
  23.9 0.3 compare_reduce_fusion.24
  24.2 15.7 %fusion.21 = s32[1024]{0:T(1024)S(1)} fusion(pred[1024]{0:T(1024)(128)(4,1)S(1)} %get-tuple-element.56, pred[1024]{0:T(1024)(128)(4,1)S(1)} %get-tuple-element.55, pred[1024]{0:T(1024)(128)(4,1)S(1)} %get-tuple-element.54, pred[1024]{0:T(1024)(128)(4,1)S(1)} %get-tuple-element.53, pred[1024]{0:T(1024)(128)(4,1)S(1)} %get-tuple-element.52, ...), kind=kLoop, calls=%fused_computation.100 | loop fusion | flops 28672 | bytes 37988 | tf_op jit(solution)/shard_map/add | solution.py:76
  39.9 4.3 %scatter_custom_fusion = s32[1024]{0:T(1024)S(1)} fusion(s32[1024]{0:T(1024)S(1)} %get-tuple-element.71, s32[1024]{0:T(1024)S(1)} %fusion.21, s32[]{:T(128)} %constant.14.clone.1), kind=kCustom, calls=%fused_computation.109 | custom fusion | bytes 4100 | tf_op jit(solution)/shard_map/scatter | solution.py:76
  44.2 0.6 broadcast_clamp_fusion.1
  44.8 4.5 %scatter_custom_fusion.1 = s32[2048]{0:T(1024)S(1)} fusion(s32[1024]{0:T(1024)S(1)} %get-tuple-element.69, s32[1024]{0:T(1024)} %param.20, s32[]{:T(128)} %constant.13.clone.1), kind=kCustom, calls=%fused_computation.101 | custom fusion | bytes 8704 | tf_op jit(solution)/shard_map/scatter | solution.py:79
  49.3 0.7 all_to_all.12
  50.0 7.1 %all-to-all-start = ((s32[32,1,64]{2,1,0:T(1,128)}), s32[32,1,64]{2,1,0:T(1,128)S(1)}, u32[]{:S(2)}, u32[]{:S(2)}) async-start(s32[32,1,64]{2,1,0:T(1,128)} %all_to_all.12), calls=%async_computation | async-start | bytes 32768 | tf_op jit(solution)/shard_map/all_to_all | solution.py:88
  57.1 2.0 gather_fusion.1
  59.1 3.5 collective-permute-start
  62.7 1.9 collective-permute-start.1
  64.7 28.8 %scatter_custom_fusion.3 = f32[1024]{0:T(1024)S(1)} fusion(s32[4096]{0:T(1024)S(1)} %bitcast.123, f32[4096]{0:T(1024)S(1)} %broadcast.241, f32[]{:T(128)} %constant.21.clone.1), kind=kCustom, calls=%fused_computation.107 | custom fusion | flops 4096 | bytes 4100 | tf_op jit(solution)/shard_map/scatter-add | solution.py:56
  93.6 16.9 %gather_fusion.2 = bf16[4096,256]{1,0:T(8,128)(2,1)} fusion(bf16[1536,256]{1,0:T(8,128)(2,1)S(1)} %pad_maximum_fusion, s32[4096]{0:T(1024)S(1)} %bitcast_clamp_fusion.1), kind=kCustom, calls=%fused_computation.2 | custom fusion | bytes 4210688 | tf_op jit(solution)/shard_map/gather | solution.py:49
  110.6 4.3 %fusion.32 = f32[4,1024,256]{2,1,0:T(8,128)} fusion(bf16[4,1024,256]{2,1,0:T(8,128)(2,1)} %bitcast.104, bf16[4,256,256]{2,1,0:T(8,128)(2,1)S(1)} %copy-done), kind=kOutput, calls=%fused_computation.115 | convolution fusion | flops 536870912 | bytes 6815744 | tf_op jit(solution)/shard_map/tek,tkd->ted/dot_general | solution.py:50
  114.8 23.3 %scatter_custom_fusion.2 = f32[1024,256]{1,0:T(8,128)S(1)} fusion(s32[4096]{0:T(1024)S(1)} %bitcast.124, f32[4096,256]{1,0:T(8,128)} %bitcast.111, f32[]{:T(128)} %constant.12.clone.1), kind=kCustom, calls=%fused_computation.37 | custom fusion | flops 1048576 | bytes 1049088 | tf_op jit(solution)/shard_map/scatter-add | solution.py:54
  138.1 0.3 convolution_add_fusion.1
  138.4 6.2 %scatter_custom_fusion.4 = bf16[2048,256]{1,0:T(8,128)(2,1)} fusion(s32[1024]{0:T(1024)S(1)} %get-tuple-element.69, f32[1024,256]{1,0:T(8,128)S(1)} %convolution_add_fusion.1, f32[]{:T(128)} %constant.21.clone.1, bf16[]{:T(256)} %constant.19.clone.1), kind=kCustom, calls=%fused_computation.31 | custom fusion | flops 1310720 | bytes 2097158 | tf_op jit(solution)/shard_map/scatter | solution.py:78
  144.7 5.9 %all-to-all-start.1 = ((bf16[32,64,256]{2,1,0:T(8,128)(2,1)}), bf16[32,64,256]{2,1,0:T(8,128)(2,1)S(1)}, u32[]{:S(2)}, u32[]{:S(2)}) async-start(bf16[32,64,256]{2,1,0:T(8,128)(2,1)} %bitcast.109), calls=%async_computation.1 | async-start | bytes 2097152 | tf_op jit(solution)/shard_map/all_to_all | solution.py:81
  150.7 0.5 broadcast.465
  151.2 0.7 reduce.54
  152.0 0.6 broadcast_clamp_fusion
  152.6 0.6 compare_and_fusion
  153.2 24.5 %all-to-all-done.1 = bf16[32,64,256]{2,1,0:T(8,128)(2,1)S(1)} async-done(((bf16[32,64,256]{2,1,0:T(8,128)(2,1)}), bf16[32,64,256]{2,1,0:T(8,128)(2,1)S(1)}, u32[]{:S(2)}, u32[]{:S(2)}) %all-to-all-start.1) | async-done | bytes 1048608 | tf_op jit(solution)/shard_map/all_to_all | solution.py:81
  177.6 11.7 %scatter_custom_fusion.5 = f32[256,256]{1,0:T(8,128)S(1)} fusion(s32[2048]{0:T(1024)S(1)} %bitcast.120, bf16[2048,256]{1,0:T(8,128)(2,1)S(1)} %bitcast.108, f32[]{:T(128)} %constant.12.clone.1), kind=kCustom, calls=%fused_computation.14 | custom fusion | flops 1048576 | bytes 1310724 | tf_op jit(solution)/shard_map/scatter-add | solution.py:101
  189.3 1.5 multiply_convert_fusion.3
  190.9 0.2 fusion.33
  191.1 0.5 copy-done.7
  191.6 0.4 multiply_convert_fusion.2
  192.0 0.2 copy-done.19
  192.2 0.8 copy-done.6
  193.0 0.3 convolution_convert_fusion
  193.4 8.5 %gather_fusion.3 = bf16[2048,256]{1,0:T(8,128)(2,1)S(1)} fusion(bf16[256,256]{1,0:T(8,128)(2,1)S(1)} %convolution_convert_fusion, s32[2048]{0:T(1024)} %broadcast_clamp_fusion), kind=kCustom, calls=%fused_computation.3 | custom fusion | bytes 2105344 | tf_op jit(solution)/shard_map/jit(_take)/gather | solution.py:116
  201.8 1.9 broadcast_select_fusion
  203.7 3.2 all-to-all-start.2
  207.1 2.4 fusion.15
  209.5 24.6 %all-to-all-done.2 = bf16[32,64,256]{2,1,0:T(8,128)(2,1)S(1)} async-done(((bf16[32,64,256]{2,1,0:T(8,128)(2,1)}), bf16[32,64,256]{2,1,0:T(8,128)(2,1)S(1)}, u32[]{:S(2)}, u32[]{:S(2)}) %all-to-all-start.2) | async-done | bytes 1048608 | tf_op jit(solution)/shard_map/all_to_all | solution.py:117
  234.1 5.0 %gather_fusion.4 = bf16[1024,256]{1,0:T(8,128)(2,1)} fusion(bf16[2048,256]{1,0:T(8,128)(2,1)S(1)} %bitcast.103, s32[1024]{0:T(1024)S(1)} %copy-done.18), kind=kCustom, calls=%fused_computation.4 | custom fusion | bytes 1052672 | tf_op jit(solution)/shard_map/gather | solution.py:124
  239.1 1.5 multiply_convert_fusion
  240.6 1.0 convolution_bitcast_fusion
  241.6 16.9 %gather_fusion.5 = bf16[4096,256]{1,0:T(8,128)(2,1)} fusion(bf16[1024,256]{1,0:T(8,128)(2,1)S(1)} %get-tuple-element.60, s32[4096]{0:T(1024)S(1)} %bitcast_clamp_fusion), kind=kCustom, calls=%fused_computation.5 | custom fusion | bytes 4210688 | tf_op jit(solution)/shard_map/gather | solution.py:128
  258.5 4.1 %fusion.35 = f32[4,256,256]{2,1,0:T(8,128)} fusion(bf16[4,1024,256]{2,1,0:T(8,128)(2,1)} %bitcast.105, bf16[4,1024,256]{2,1,0:T(8,128)(2,1)} %bitcast.106), kind=kOutput, calls=%fused_computation.118 | convolution fusion | flops 536870912 | bytes 5242880 | tf_op jit(solution)/shard_map/tek,ted->tkd/dot_general | solution.py:129
  262.7 0.6 copy-done.20
  263.3 0.3 fusion.36
  263.6 37.8 %psum.31 = f32[1024]{0:T(1024)S(1)} all-reduce(f32[1024]{0:T(1024)S(1)} %bitcast.121), channel_id=1, replica_groups=mesh['group'=4,'dom'=8] {'group','dom'}, use_global_device_ids=true, to_apply=%region_14.15 | all-reduce | flops 1024 | bytes 8192 | tf_op jit(solution)/shard_map/psum | solution.py:146
  301.4 0.6 broadcast_multiply_fusion.3
  302.0 2.7 fusion.34
  304.7 23.3 %scatter_custom_fusion.6 = f32[1536,256]{1,0:T(8,128)S(1)} fusion(s32[4096]{0:T(1024)S(1)} %bitcast.122, f32[4096,256]{1,0:T(8,128)} %bitcast.110, f32[]{:T(128)} %constant.12.clone.1), kind=kCustom, calls=%fused_computation.29 | custom fusion | flops 1048576 | bytes 1573376 | tf_op jit(solution)/shard_map/scatter-add | solution.py:136
  328.1 4.8 %collective-permute-start.2 = (bf16[256,256]{1,0:T(8,128)(2,1)S(1)}, bf16[256,256]{1,0:T(8,128)(2,1)S(1)}, u32[]{:S(2)}, u32[]{:S(2)}) collective-permute-start(bf16[256,256]{1,0:T(8,128)(2,1)S(1)} %get-tuple-element.64), channel_id=1, source_target_pairs={{0,1},{1,2},{2,3},{3,4},{4,5},{5,6},{6,7},{8,9},{9,10},{10,11},{11... | collective-permute-start | bytes 393224 | tf_op jit(solution)/shard_map/ppermute | solution.py:14
  332.9 1.9 collective-permute-start.3
  334.9 1.3 convolution_add_fusion
  336.2 3.7 collective-permute-done.3
  339.8 5.3 %scatter_custom_fusion.7 = f32[1024,256]{1,0:T(8,128)} fusion(f32[1024,256]{1,0:T(8,128)} %convolution_add_fusion, s32[512]{0:T(512)} %bitcast.128, bf16[256,256]{1,0:T(8,128)(2,1)S(1)} %collective-permute-done.3, bf16[]{:T(256)} %constant.123, bf16[256,256]{1,0:T(8,128)(2,1)S(1)} %collective-permute-done.2), kind=kCustom, calls=%fused_computation.34 | custom fusion | flops 655360 | bytes 1311232 | tf_op jit(solution)/shard_map/scatter-add | solution.py:145
  345.2 2.1 convert_element_type.61
  347.3 48.5 %all-reduce.3.cloned.1.call-done = (f32[256,256]{0,1:T(8,128)}, f32[4,256,256]{2,1,0:T(8,128)}, f32[256,1024]{1,0:T(8,128)}) async-done(((f32[256,256]{0,1:T(8,128)}, f32[4,256,256]{2,1,0:T(8,128)}, f32[256,1024]{1,0:T(8,128)}), (f32[256,256]{0,1:T(8,128)}, f32[4,256,256]{2,1,0:T(8,128)}, f32[256,1024]{1,0:T(8,128)})) %all-reduce.3.cloned.1.call-update) | async-done | bytes 2359312 | tf_op jit(solution)/shard_map/psum | solution.py:146
  395.8 1.1 broadcast_multiply_fusion.2
  396.9 0.8 copy.28
  397.7 2.3 broadcast_multiply_fusion.1
  400.0 1.1 broadcast_multiply_fusion
  (80 shorter events, 0.8 us)
Async XLA Ops:
  7.2 103.4 %copy-start = (bf16[4,256,256]{2,1,0:T(8,128)(2,1)S(1)}, bf16[4,256,256]{2,1,0:T(8,128)(2,1)}, u32[]{:S(2)}) copy-start(bf16[4,256,256]{2,1,0:T(8,128)(2,1)} %param.13) | copy-start | bytes 1572868
  7.2 7.7 %copy-start.1 = (s32[1024,1]{0,1:T(1,128)S(1)}, s32[1024,1]{0,1:T(1,128)}, u32[]{:S(2)}) copy-start(s32[1024,1]{0,1:T(1,128)} %param.19) | copy-start | bytes 12292
  14.9 42.2 %copy-start.24 = (s32[1,512]{1,0:T(1,128)S(1)}, s32[1,512]{1,0:T(1,128)}, u32[]{:S(2)}) copy-start(s32[1,512]{1,0:T(1,128)} %param.16) | copy-start | bytes 6148
  14.9 42.3 %copy-start.2 = (bf16[1024,256]{1,0:T(8,128)(2,1)S(1)}, bf16[1024,256]{1,0:T(8,128)(2,1)}, u32[]{:S(2)}) copy-start(bf16[1024,256]{1,0:T(8,128)(2,1)} %param.11) | copy-start | bytes 1572868
  19.4 45.2 %copy-start.14 = (s32[1,4,1024]{2,1,0:T(4,128)S(1)}, s32[1,4,1024]{2,1,0:T(4,128)}, u32[]{:S(2)}) copy-start(s32[1,4,1024]{2,1,0:T(4,128)} %param.18) | copy-start | bytes 49156
  19.4 45.2 %copy-start.13 = (s32[1,4,1024]{2,1,0:T(4,128)S(1)}, s32[1,4,1024]{2,1,0:T(4,128)}, u32[]{:S(2)}) copy-start(s32[1,4,1024]{2,1,0:T(4,128)} %param.17) | copy-start | bytes 49156
  50.0 94.7 %all-to-all-start = ((s32[32,1,64]{2,1,0:T(1,128)}), s32[32,1,64]{2,1,0:T(1,128)S(1)}, u32[]{:S(2)}, u32[]{:S(2)}) async-start(s32[32,1,64]{2,1,0:T(1,128)} %all_to_all.12), calls=%async_computation | async-start | bytes 32768 | tf_op jit(solution)/shard_map/all_to_all | solution.py:88
  57.1 7.5 %copy-start.22 = (s32[512,1]{0,1:T(1,128)}, s32[512,1]{0,1:T(1,128)S(1)}, u32[]{:S(2)}) copy-start(s32[512,1]{0,1:T(1,128)S(1)} %compare_select_fusion.13) | copy-start | bytes 6148
  59.1 34.4 %collective-permute-start = (bf16[256,256]{1,0:T(8,128)(2,1)S(1)}, bf16[256,256]{1,0:T(8,128)(2,1)S(1)}, u32[]{:S(2)}, u32[]{:S(2)}) collective-permute-start(bf16[256,256]{1,0:T(8,128)(2,1)S(1)} %get-tuple-element.66), channel_id=1, source_target_pairs={{0,1},{1,2},{2,3},{3,4},{4,5},{5,6},{6,7},{8,9},{9,10},{10,11},{11... | collective-permute-start | bytes 393224 | tf_op jit(solution)/shard_map/ppermute | solution.py:14
  62.7 30.9 %collective-permute-start.1 = (bf16[256,256]{1,0:T(8,128)(2,1)S(1)}, bf16[256,256]{1,0:T(8,128)(2,1)S(1)}, u32[]{:S(2)}, u32[]{:S(2)}) collective-permute-start(bf16[256,256]{1,0:T(8,128)(2,1)S(1)} %get-tuple-element.67), channel_id=1, source_target_pairs={{1,0},{2,1},{3,2},{4,3},{5,4},{6,5},{7,6},{9,8},{10,9},{11,10},{12... | collective-permute-start | bytes 393224 | tf_op jit(solution)/shard_map/ppermute | solution.py:17
  93.5 44.6 %copy-start.16 = (f32[1024]{0:T(1024)}, f32[1024]{0:T(1024)S(1)}, u32[]{:S(2)}) copy-start(f32[1024]{0:T(1024)S(1)} %broadcast_divide_fusion) | copy-start | bytes 12292
  110.6 27.6 %copy-start.11 = (bf16[256,256]{1,0:T(8,128)(2,1)S(1)}, bf16[256,256]{1,0:T(8,128)(2,1)}, u32[]{:S(2)}) copy-start(bf16[256,256]{1,0:T(8,128)(2,1)} %param.12) | copy-start | bytes 393220
  138.4 12.2 %copy-start.21 = (bf16[1024]{0:T(1024)(128)(2,1)S(1)}, bf16[1024]{0:T(1024)(128)(2,1)}, u32[]{:S(2)}) copy-start(bf16[1024]{0:T(1024)(128)(2,1)} %param.15) | copy-start | bytes 6148
  144.7 32.9 %all-to-all-start.1 = ((bf16[32,64,256]{2,1,0:T(8,128)(2,1)}), bf16[32,64,256]{2,1,0:T(8,128)(2,1)S(1)}, u32[]{:S(2)}, u32[]{:S(2)}) async-start(bf16[32,64,256]{2,1,0:T(8,128)(2,1)} %bitcast.109), calls=%async_computation.1 | async-start | bytes 2097152 | tf_op jit(solution)/shard_map/all_to_all | solution.py:81
  189.3 1.8 copy-start.25
  190.8 0.8 copy-start.7
  190.8 2.2 copy-start.10
  191.1 0.9 copy-start.23
  191.6 0.6 copy-start.19
  192.2 0.8 copy-start.6
  203.7 3.3 copy-start.15
  203.7 30.4 %copy-start.18 = (s32[1024]{0:T(1024)S(1)}, s32[1024]{0:T(1024)}, u32[]{:S(2)}) copy-start(s32[1024]{0:T(1024)} %get-tuple-element.68) | copy-start | bytes 12292
  203.7 30.4 %all-to-all-start.2 = ((bf16[32,64,256]{2,1,0:T(8,128)(2,1)}), bf16[32,64,256]{2,1,0:T(8,128)(2,1)S(1)}, u32[]{:S(2)}, u32[]{:S(2)}) async-start(bf16[32,64,256]{2,1,0:T(8,128)(2,1)} %broadcast_select_fusion), calls=%async_computation.2 | async-start | bytes 2097152 | tf_op jit(solution)/shard_map/all_to_all | solution.py:117
  207.0 188.8 %all-reduce.3.cloned.1.call-start = ((), (), s32[]{:S(2)}) async-start(), calls=%async_computation.3 | async-start | bytes 4718592 | tf_op jit(solution)/shard_map/psum | solution.py:146
  234.1 5.0 %copy-start.17 = (f32[1024]{0:T(1024)S(1)}, f32[1024]{0:T(1024)}, u32[]{:S(2)}) copy-start(f32[1024]{0:T(1024)} %copy-done.16) | copy-start | bytes 12292
  240.6 18.0 %copy-start.4 = (bf16[1024,256]{1,0:T(8,128)(2,1)}, bf16[1024,256]{1,0:T(8,128)(2,1)S(1)}, u32[]{:S(2)}) copy-start(bf16[1024,256]{1,0:T(8,128)(2,1)S(1)} %get-tuple-element.61) | copy-start | bytes 1572868
  258.5 4.1 %copy-start.8 = (bf16[256,1024]{1,0:T(8,128)(2,1)S(1)}, bf16[256,1024]{1,0:T(8,128)(2,1)}, u32[]{:S(2)}) copy-start(bf16[256,1024]{1,0:T(8,128)(2,1)} %copy-done.7) | copy-start | bytes 1572868
  262.7 0.7 copy-start.20
  262.7 39.4 %copy-start.3 = (bf16[4096,256]{1,0:T(8,128)(2,1)S(1)}, bf16[4096,256]{1,0:T(8,128)(2,1)}, u32[]{:S(2)}) copy-start(bf16[4096,256]{1,0:T(8,128)(2,1)} %gather_fusion.5) | copy-start | bytes 6291460
  304.7 30.1 %copy-start.5 = (bf16[1024,256]{1,0:T(8,128)(2,1)S(1)}, bf16[1024,256]{1,0:T(8,128)(2,1)}, u32[]{:S(2)}) copy-start(bf16[1024,256]{1,0:T(8,128)(2,1)} %copy-done.4) | copy-start | bytes 1572868
  304.7 30.2 %copy-start.12 = (bf16[256,256]{1,0:T(8,128)(2,1)S(1)}, bf16[256,256]{1,0:T(8,128)(2,1)}, u32[]{:S(2)}) copy-start(bf16[256,256]{1,0:T(8,128)(2,1)} %param.12) | copy-start | bytes 393220
  328.1 8.1 %collective-permute-start.2 = (bf16[256,256]{1,0:T(8,128)(2,1)S(1)}, bf16[256,256]{1,0:T(8,128)(2,1)S(1)}, u32[]{:S(2)}, u32[]{:S(2)}) collective-permute-start(bf16[256,256]{1,0:T(8,128)(2,1)S(1)} %get-tuple-element.64), channel_id=1, source_target_pairs={{0,1},{1,2},{2,3},{3,4},{4,5},{5,6},{6,7},{8,9},{9,10},{10,11},{11... | collective-permute-start | bytes 393224 | tf_op jit(solution)/shard_map/ppermute | solution.py:14
  332.9 6.9 %collective-permute-start.3 = (bf16[256,256]{1,0:T(8,128)(2,1)S(1)}, bf16[256,256]{1,0:T(8,128)(2,1)S(1)}, u32[]{:S(2)}, u32[]{:S(2)}) collective-permute-start(bf16[256,256]{1,0:T(8,128)(2,1)S(1)} %get-tuple-element.65), channel_id=1, source_target_pairs={{1,0},{2,1},{3,2},{4,3},{5,4},{6,5},{7,6},{9,8},{10,9},{11,10},{12... | collective-permute-start | bytes 393224 | tf_op jit(solution)/shard_map/ppermute | solution.py:17
  395.8 4.2 %copy-start.9 = (f32[256,1024]{1,0:T(8,128)S(1)}, f32[256,1024]{1,0:T(8,128)}, u32[]{:S(2)}) copy-start(f32[256,1024]{1,0:T(8,128)} %get-tuple-element.59) | copy-start | bytes 3145732
Sparse Core Ops, SparseCore 0:
  262.8 132.9 all-reduce.2
where the time goes:
time: 411 us; the launch traced here: 408 us
  other arithmetic  139 us (34%)
  waiting for transfers between devices  101 us (25%)
  local copies, waits for them, and re-layouts  68.5 us (17%)
  blocking collectives  37.8 us (9%)
  starting transfers between devices  28.5 us (7%)
  matrix products  18.4 us (4%)
  between operations  14.6 us (4%)
    psum x1, waiting for transfers between devices, on_device(): totals = lax.psum((self_sum, edge_sum, head_sum, out_sum), ('group', 'dom'))  48.5 us
    psum x1, blocking collectives, on_device(): totals = lax.psum((self_sum, edge_sum, head_sum, out_sum), ('group', 'dom'))  37.8 us
    scatter-add x1, other arithmetic, on_device(): degree = jnp.zeros((pin_count,), jnp.float32).at[flat_end].add(1.0)  28.8 us
    all_to_all x1, waiting for transfers between devices, on_device(): lax.all_to_all(returned.reshape(owners, capacity, feat_width), ('group',...  24.6 us
    all_to_all x1, waiting for transfers between devices, on_device(): lax.all_to_all(outbound.reshape(owners, capacity, feat_width), ('group',...  24.5 us
    scatter-add x1, other arithmetic, on_device(): table_grad = jnp.zeros((node_table.shape[0], feat_width), jnp.float32).at...  23.3 us
    scatter-add x1, other arithmetic, on_device(): summed = jnp.zeros((pin_count, feat_width), jnp.float32).at[flat_end].add...  23.3 us
    gather x1, local copies, waits for them, and re-layouts, on_device(): gathered = node_table[sources]  16.9 us
  transfers between devices with their start and end apart: 8, of which 4 were waited for; matrix products, arithmetic and copies ran while one was open for 30% of the time, Pallas kernels for 0%

commit v1 on v0

v1 whole, which is shorter than its diff:
```python
import math

import jax
import jax.numpy as jnp
from jax import lax
from jax.sharding import PartitionSpec as P


F32 = jnp.float32
BF16 = jnp.bfloat16


def extended(block, sides, width):
    for axis, dim in sides:
        count = lax.axis_size(axis)
        forward = [(i, i + 1) for i in range(count - 1)]
        backward = [(target, source) for source, target in forward]
        low = lax.ppermute(
            lax.slice_in_dim(block, block.shape[dim] - width, None, axis=dim), axis, forward
        )
        high = lax.ppermute(lax.slice_in_dim(block, 0, width, axis=dim), axis, backward)
        block = jnp.concatenate([low, block, high], axis=dim)
    return block


def silu_slope(values):
    sigma_val = jax.nn.sigmoid(values)
    return sigma_val * (1.0 + values * (1.0 - sigma_val))


def one_hot(index, count):
    return (index[..., None] == jnp.arange(count, dtype=index.dtype)).astype(BF16)


def split_dot(spec, left, right):
    head = left.astype(BF16)
    tail = (left - head.astype(F32)).astype(BF16)
    return jnp.einsum(spec, head, right, preferred_element_type=F32) + jnp.einsum(
        spec, tail, right, preferred_element_type=F32
    )


def on_device(
    pin_feats,
    w_self,
    w_edge,
    w_head,
    w_out,
    send_rows,
    edge_src,
    edge_dst,
    pin_owner,
    pin_net,
    net_target,
):
    pin_count, feat_width = pin_feats.shape
    send_list = send_rows[0]
    halo_span = send_list.shape[0] // 2
    send_hot = one_hot(send_list, pin_count)
    outgoing = jnp.dot(send_hot, pin_feats, preferred_element_type=F32).astype(BF16)
    padded = extended(outgoing, (("dom", 0),), halo_span)
    node_table = jnp.concatenate([pin_feats, padded[:halo_span], padded[3 * halo_span :]], 0)
    table_rows = node_table.shape[0]
    sources = edge_src[0]
    endpoints = edge_dst[0]
    src_hot = one_hot(sources, table_rows)
    dst_hot = one_hot(endpoints, pin_count)
    gathered = jnp.einsum(
        "ter,rd->ted", src_hot, node_table, preferred_element_type=F32
    ).astype(BF16)
    edge_in = jnp.einsum("tep,ted->tpd", dst_hot, gathered, preferred_element_type=F32)
    summed = split_dot("tpk,tkd->pd", edge_in, w_edge)
    degree = jnp.sum(dst_hot.astype(F32), axis=(0, 1))
    inverse = 1.0 / (1.0 + degree)
    preact = (
        jnp.dot(pin_feats, w_self, preferred_element_type=F32) + summed * inverse[:, None]
    )
    hidden = jax.nn.silu(preact).astype(BF16)
    groups = lax.axis_size("group")
    domains = lax.axis_size("dom")
    owners = groups * domains
    capacity = max(2, 2 * pin_count // owners)
    net_count = net_target.shape[0]
    owner_ids = pin_owner[:, 0]
    owner_hot = one_hot(owner_ids, owners)
    earlier = (
        jnp.arange(pin_count, dtype=jnp.int32)[None, :]
        < jnp.arange(pin_count, dtype=jnp.int32)[:, None]
    ).astype(BF16)
    before = jnp.dot(earlier, owner_hot, preferred_element_type=F32)
    slot_rank = jnp.sum(before * owner_hot.astype(F32), axis=1).astype(jnp.int32)
    pin_slot = owner_ids * capacity + slot_rank
    slot_hot = one_hot(pin_slot, owners * capacity)
    net_code = (pin_net + 1).astype(BF16)[:, None]
    slot_nets = (
        jnp.dot(slot_hot.T, net_code, preferred_element_type=F32)[:, 0].astype(jnp.int32) - 1
    )
    slot_nets_in = lax.all_to_all(
        slot_nets.reshape(owners, capacity),
        ("group", "dom"),
        split_axis=0,
        concat_axis=0,
        tiled=True,
    ).reshape(-1)
    outbound = jnp.dot(slot_hot.T, hidden, preferred_element_type=F32).astype(BF16)
    inbound = lax.all_to_all(
        outbound.reshape(owners, capacity, feat_width),
        ("group", "dom"),
        split_axis=0,
        concat_axis=0,
        tiled=True,
    ).reshape(-1, feat_width)
    net_hot = one_hot(slot_nets_in, net_count)
    pooled = jnp.einsum("sn,sd->nd", net_hot, inbound, preferred_element_type=F32)
    pooled_b = pooled.astype(BF16)
    head_pre = jnp.dot(pooled_b, w_head, preferred_element_type=F32)
    activated = jax.nn.silu(head_pre).astype(BF16)
    predicted = jnp.dot(activated, w_out, preferred_element_type=F32)
    misfit = predicted - net_target
    head_grad = (
        misfit[:, None] * w_out.astype(F32)[None, :] * silu_slope(head_pre)
    ).astype(BF16)
    head_sum = jnp.einsum("nd,nh->dh", pooled_b, head_grad, preferred_element_type=F32)
    out_sum = jnp.dot(misfit, activated.astype(F32), precision=lax.Precision.HIGHEST)
    head_totals = lax.psum((head_sum, out_sum), ("group", "dom"))
    net_grad = jnp.einsum(
        "nh,dh->nd", head_grad, w_head, preferred_element_type=F32
    ).astype(BF16)
    returned = jnp.dot(net_hot, net_grad, preferred_element_type=F32).astype(BF16)
    arrived = lax.all_to_all(
        returned.reshape(owners, capacity, feat_width),
        ("group", "dom"),
        split_axis=0,
        concat_axis=0,
        tiled=True,
    ).reshape(-1, feat_width)
    pin_grad = jnp.dot(slot_hot, arrived, preferred_element_type=F32)
    preact_grad = (pin_grad * silu_slope(preact)).astype(BF16)
    self_sum = jnp.einsum("pk,pd->kd", pin_feats, preact_grad, preferred_element_type=F32)
    agg_grad = (preact_grad.astype(F32) * inverse[:, None]).astype(BF16)
    edge_rows = jnp.einsum(
        "tep,pd->ted", dst_hot, agg_grad, preferred_element_type=F32
    ).astype(BF16)
    edge_sum = jnp.einsum("tek,ted->tkd", gathered, edge_rows, preferred_element_type=F32)
    row_in = jnp.einsum("ter,ted->trd", src_hot, edge_rows, preferred_element_type=F32)
    table_grad = split_dot("trd,tkd->rk", row_in, w_edge)
    local_grad = (
        jnp.einsum("pd,kd->pk", preact_grad, w_self, preferred_element_type=F32)
        + table_grad[:pin_count]
    )
    halo_grad = table_grad[pin_count:].astype(BF16)
    back_padded = extended(halo_grad, (("dom", 0),), halo_span)
    received = jnp.concatenate([back_padded[:halo_span], back_padded[3 * halo_span :]], 0)
    grad_feats = (
        local_grad + jnp.einsum("sp,sd->pd", send_hot, received, preferred_element_type=F32)
    ).astype(BF16)
    tail_totals = lax.psum((self_sum, edge_sum), ("group", "dom"))
    grad_scale = 1.0 / math.sqrt(pin_count * owners)
    return (
        predicted,
        grad_feats,
        tail_totals[0] * grad_scale,
        tail_totals[1] * grad_scale,
        head_totals[0] * grad_scale,
        head_totals[1] * grad_scale,
    )


def solution(mesh):
    in_specs = (
        P(("group", "dom"), None),
        P(),
        P(),
        P(),
        P(),
        P(("group", "dom"), None),
        P(("group", "dom"), None, None),
        P(("group", "dom"), None, None),
        P(("group", "dom"), None),
        P(("group", "dom")),
        P(("group", "dom")),
    )
    out_specs = (P(("group", "dom")), P(("group", "dom"), None), P(), P(), P(), P())
    return jax.shard_map(
        on_device, mesh=mesh, in_specs=in_specs, out_specs=out_specs, check_vma=False
    )
```

time: 411 us -> 312 us (0.76)
  other arithmetic: 139 us -> 10.4 us
  local copies, waits for them, and re-layouts: 68.5 us -> 7.33 us
  waiting for transfers between devices: 101 us -> 153 us
  matrix products: 18.4 us -> 53.2 us
  blocking collectives: 37.8 us -> 45 us
    scatter-add x5 -> x0, other arithmetic: 92.4 us -> none  [the longest x1 28.8 us: on_device(): degree = jnp.zeros((pin_count,), jnp.float32).at[flat_end].add(1.0)]
    psum x1, waiting for transfers between devices: 48.5 us -> 120 us  [on_device(): tail_totals = lax.psum((self_sum, edge_sum), ('group', 'dom'))]
    gather x8 -> x0, local copies, waits for them, and re-layouts: 55.2 us -> none  [the longest x1 16.9 us: on_device(): gathered = node_table[sources]]
    dot_general x11 -> x24, matrix products: 18.4 us -> 53.2 us  [the longest x1 6.92 us: on_device(): jnp.einsum('ter,rd->ted', src_hot, node_table, preferred_element_type=F32)]
    all_to_all x1, waiting for transfers between devices: 24.6 us -> 0.01 us  [on_device(): lax.all_to_all(returned.reshape(owners, capacity, feat_width), ('group',...]
    add x1, other arithmetic: 15.7 us -> 0.7 us  [on_device(): pin_slot = owner_ids * capacity + slot_rank]
    scatter x2 -> x0, local copies, waits for them, and re-layouts: 8.78 us -> none  [the longest x1 4.47 us: on_device(): jnp.full((owners * capacity,), net_count, jnp.int32).at[pin_slot]]
    psum x1, blocking collectives: 37.8 us -> 45 us  [on_device(): head_totals = lax.psum((head_sum, out_sum), ('group', 'dom'))]
  transfers between devices with their start and end apart: 8 -> 8, of which waited for: 4 -> 5; matrix products, arithmetic and copies ran while one was open for 30% -> 10% of each run, Pallas kernels for 0% -> 0%
where the time goes in v1:
time: 312 us; the launch traced here: 310 us
  waiting for transfers between devices  153 us (49%)
  matrix products  53.2 us (17%)
  blocking collectives  45 us (14%)
  starting transfers between devices  25.9 us (8%)
  between operations  14.4 us (5%)
  other arithmetic  10.4 us (3%)
  local copies, waits for them, and re-layouts  7.33 us (2%)
    psum x1, waiting for transfers between devices, on_device(): tail_totals = lax.psum((self_sum, edge_sum), ('group', 'dom'))  120 us
    psum x1, blocking collectives, on_device(): head_totals = lax.psum((head_sum, out_sum), ('group', 'dom'))  45 us
    all_to_all x1, waiting for transfers between devices, on_device(): lax.all_to_all(outbound.reshape(owners, capacity, feat_width), ('group',...  25.7 us
    all_to_all x1, starting transfers between devices, on_device(): lax.all_to_all(slot_nets.reshape(owners, capacity), ('group', 'dom'), spl...  7.1 us
    dot_general x1, matrix products, on_device(): jnp.einsum('ter,rd->ted', src_hot, node_table, preferred_element_type=F32)  6.92 us
    ppermute x2, waiting for transfers between devices, extended(): lax.ppermute(lax.slice_in_dim(block, 0, width, axis=dim), axis, backward)  6.72 us
    ppermute x2, starting transfers between devices, extended(): lax.ppermute(lax.slice_in_dim(block, block.shape[dim] - width, None, axis...  6.43 us
  transfers between devices with their start and end apart: 8, of which 5 were waited for; matrix products, arithmetic and copies ran while one was open for 10% of the time, Pallas kernels for 0%

profile of v1, /device:TPU:1, one launch (start us, length us, event | category | flops | bytes accessed | tf_op | source)
XLA Modules:
  0.0 309.5 jit_solution(8071651722822437090)
XLA Ops:
  7.2 0.0 copy-start
  7.2 0.0 copy-start.3
  7.2 0.8 add_convert_fusion
  8.0 1.3 fusion.38
  9.3 0.0 copy-start.11
  9.3 0.0 copy-start.12
  9.3 0.7 multiply_add_fusion
  10.0 1.5 fusion.11
  11.5 0.7 sub.22
  12.2 7.1 %all-to-all-start = ((s32[32,1,64]{2,1,0:T(1,128)}), s32[32,1,64]{2,1,0:T(1,128)S(1)}, u32[]{:S(2)}, u32[]{:S(2)}) async-start(s32[32,1,64]{2,1,0:T(1,128)} %sub.22), calls=%async_computation | async-start | bytes 32768 | tf_op jit(solution)/shard_map/all_to_all | solution.py:98
  19.3 0.5 fusion.35
  19.9 3.5 %collective-permute-start = (bf16[256,256]{1,0:T(8,128)(2,1)S(1)}, bf16[256,256]{1,0:T(8,128)(2,1)S(1)}, u32[]{:S(2)}, u32[]{:S(2)}) collective-permute-start(bf16[256,256]{1,0:T(8,128)(2,1)S(1)} %get-tuple-element.17), channel_id=1, source_target_pairs={{0,1},{1,2},{2,3},{3,4},{4,5},{5,6},{6,7},{8,9},{9,10},{10,11},{11... | collective-permute-start | bytes 393224 | tf_op jit(solution)/shard_map/ppermute | solution.py:18
  23.4 2.1 collective-permute-start.1
  25.5 1.9 convert_reduce_fusion
  27.5 0.0 collective-permute-done
  27.5 2.2 collective-permute-done.1
  29.7 6.9 %fusion.24 = bf16[4,1024,256]{2,1,0:T(8,128)(2,1)S(1)} fusion(s32[4,1024]{1,0:T(4,128)S(1)} %bitcast.79, bf16[256,256]{1,0:T(8,128)(2,1)S(1)} %collective-permute-done.1, bf16[256,256]{1,0:T(8,128)(2,1)S(1)} %collective-permute-done, bf16[1024,256]{1,0:T(8,128)(2,1)S(1)} %copy-done.3), kind=kOutput, calls=%fused_computation.35 | convolution fusion | flops 3230924800 | bytes 2899968 | tf_op jit(solution)/shard_map/ter,rd->ted/dot_general | solution.py:68
  36.6 5.7 %fusion.4 = f32[4,1024,256]{2,1,0:T(8,128)S(1)} fusion(bf16[4,1024,256]{2,1,0:T(8,128)(2,1)S(1)} %fusion.24, s32[4,1024]{1,0:T(4,128)S(1)} %bitcast.77), kind=kOutput, calls=%fused_computation.7 | convolution fusion | flops 2151677952 | bytes 6307840 | tf_op jit(solution)/shard_map/tep,ted->tpd/dot_general | solution.py:71
  42.4 0.7 convolution_bitcast_fusion.1
  43.1 0.0 copy-start.7
  43.1 0.7 fusion.32
  43.9 0.2 copy-done.7
  44.0 0.3 convolution_add_fusion.1
  44.3 0.0 copy-start.5
  44.3 1.0 copy-done.5
  45.3 3.5 %fusion.19 = bf16[2048,256]{1,0:T(8,128)(2,1)} fusion(s32[1024]{0:T(1024)S(1)} %bitcast.74, f32[1024,256]{1,0:T(8,128)S(1)} %convolution_add_fusion.1), kind=kOutput, calls=%fused_computation.27 | convolution fusion | flops 1077673984 | bytes 2101248 | tf_op jit(solution)/shard_map/dot_general | solution.py:105
  48.8 4.5 %all-to-all-start.1 = ((bf16[32,64,256]{2,1,0:T(8,128)(2,1)}), bf16[32,64,256]{2,1,0:T(8,128)(2,1)}, u32[]{:S(2)}, u32[]{:S(2)}) async-start(bf16[32,64,256]{2,1,0:T(8,128)(2,1)} %bitcast.64), calls=%async_computation.1 | async-start | bytes 2097152 | tf_op jit(solution)/shard_map/all_to_all | solution.py:106
  53.4 0.5 broadcast.40
  53.9 0.7 reduce.3
  54.6 0.1 eq.98
  54.7 25.7 %all-to-all-done.1 = bf16[32,64,256]{2,1,0:T(8,128)(2,1)} async-done(((bf16[32,64,256]{2,1,0:T(8,128)(2,1)}), bf16[32,64,256]{2,1,0:T(8,128)(2,1)}, u32[]{:S(2)}, u32[]{:S(2)}) %all-to-all-start.1) | async-done | bytes 1048608 | tf_op jit(solution)/shard_map/all_to_all | solution.py:106
  80.4 2.3 fusion.36
  82.7 0.0 copy-start.10
  82.7 1.5 multiply_convert_fusion.2
  84.2 0.2 fusion.64
  84.5 1.2 multiply_convert_fusion.1
  85.7 3.2 %convolution_convert_fusion = bf16[2048,256]{1,0:T(8,128)(2,1)} fusion(bf16[256,1024]{1,0:T(8,128)(2,1)} %multiply_convert_fusion.1, bf16[256,1024]{1,0:T(8,128)(2,1)} %param.14, s32[2048]{0:T(1024)S(1)} %eq.98), kind=kOutput, calls=%fused_computation.28 | convolution fusion | flops 403767296 | bytes 2105344 | tf_op jit(solution)/shard_map/dot_general | solution.py:129
  88.8 3.8 %all-to-all-start.2 = ((bf16[32,64,256]{2,1,0:T(8,128)(2,1)}), bf16[32,64,256]{2,1,0:T(8,128)(2,1)}, u32[]{:S(2)}, u32[]{:S(2)}) async-start(bf16[32,64,256]{2,1,0:T(8,128)(2,1)} %bitcast.65), calls=%async_computation.2 | async-start | bytes 2097152 | tf_op jit(solution)/shard_map/all_to_all | solution.py:130
  92.6 0.0 all-reduce.3.cloned.1.call-start
  92.6 0.3 fusion.67
  93.0 45.0 %psum.31 = f32[1024]{0:T(1024)S(1)} all-reduce(f32[1024]{0:T(1024)S(1)} %bitcast.66), channel_id=1, replica_groups=mesh['group'=4,'dom'=8] {'group','dom'}, use_global_device_ids=true, to_apply=%region_5.6 | all-reduce | flops 1024 | bytes 8192 | tf_op jit(solution)/shard_map/psum | solution.py:125
  138.0 0.6 broadcast_multiply_fusion.3
  138.6 2.3 fusion.66
  140.9 3.3 %fusion.33 = bf16[1024,256]{1,0:T(8,128)(2,1)S(1)} fusion(bf16[2048,256]{1,0:T(8,128)(2,1)} %bitcast.14, s32[1024]{0:T(1024)S(1)} %bitcast.75, f32[1024,256]{1,0:T(8,128)} %copy-done.5), kind=kOutput, calls=%fused_computation.47 | convolution fusion | flops 1078198272 | bytes 2625536 | tf_op jit(solution)/shard_map/dot_general | solution.py:137
  144.3 1.0 convolution_bitcast_fusion.2
  145.3 3.3 %fusion.25 = bf16[4,1024,256]{2,1,0:T(8,128)(2,1)S(1)} fusion(s32[4,1024]{1,0:T(4,128)S(1)} %bitcast.78, bf16[1024,256]{1,0:T(8,128)(2,1)S(1)} %fusion.33, f32[1024]{0:T(1024)S(1)} %add_divide_fusion.2), kind=kOutput, calls=%fused_computation.36 | convolution fusion | flops 2153512960 | bytes 2641920 | tf_op jit(solution)/shard_map/tep,pd->ted/dot_general | solution.py:141
  148.6 1.3 copy-done.2
  150.0 1.9 fusion.65
  151.8 5.8 %fusion = f32[4,1536,256]{2,1,0:T(8,128)S(1)} fusion(bf16[4,1024,256]{2,1,0:T(8,128)(2,1)} %copy-done.2, s32[4,1024]{1,0:T(4,128)S(1)} %bitcast.80), kind=kOutput, calls=%fused_computation.1 | convolution fusion | flops 3227516928 | bytes 8404992 | tf_op jit(solution)/shard_map/ter,ted->trd/dot_general | solution.py:145
  157.7 2.6 copy-done.1
  160.3 1.0 fusion.17
  161.4 0.0 all-reduce.3.cloned.1.call-update
  161.4 3.8 %fusion.63 = (bf16[1536,256]{1,0:T(8,128)(2,1)S(1)}, f32[1536,256]{1,0:T(8,128)S(1)}) fusion(f32[1536,256]{1,0:T(8,128)S(1)} %fusion.17, bf16[4,256,256]{2,1,0:T(8,128)(2,1)S(1)} %copy-done, f32[4,1536,256]{2,1,0:T(8,128)} %copy-done.1), kind=kOutput, calls=%fused_computation.94 | convolution fusion | flops 807665664 | bytes 10747904 | tf_op jit(solution)/shard_map/trd,tkd->rk/dot_general | solution.py:38
  165.2 2.9 collective-permute-start.2
  168.1 1.9 collective-permute-start.3
  170.1 0.3 convolution_add_fusion
  170.4 0.4 collective-permute-done.2
  170.9 4.5 %collective-permute-done.3 = bf16[256,256]{1,0:T(8,128)(2,1)S(1)} collective-permute-done((bf16[256,256]{1,0:T(8,128)(2,1)S(1)}, bf16[256,256]{1,0:T(8,128)(2,1)S(1)}, u32[]{:S(2)}, u32[]{:S(2)}) %collective-permute-start.3) | collective-permute-done | bytes 131104 | tf_op jit(solution)/shard_map/ppermute | solution.py:21
  175.4 1.6 fusion.34
  177.0 120.4 %all-reduce.3.cloned.1.call-done = (f32[256,256]{0,1:T(8,128)}, f32[4,256,256]{2,1,0:T(8,128)}, f32[256,1024]{1,0:T(8,128)}) async-done(((f32[256,256]{0,1:T(8,128)}, f32[4,256,256]{2,1,0:T(8,128)}, f32[256,1024]{1,0:T(8,128)}), (f32[256,256]{0,1:T(8,128)}, f32[4,256,256]{2,1,0:T(8,128)}, f32[256,1024]{1,0:T(8,128)})) %all-reduce.3.cloned.1.call-update) | async-done | bytes 2359312 | tf_op jit(solution)/shard_map/psum | solution.py:157
  297.4 1.1 broadcast_multiply_fusion.2
  298.5 0.8 copy.20
  299.3 2.3 broadcast_multiply_fusion.1
  301.6 1.1 broadcast_multiply_fusion
  (28 shorter events, 0.1 us)
Async XLA Ops:
  7.2 35.2 %copy-start = (bf16[4,256,256]{2,1,0:T(8,128)(2,1)S(1)}, bf16[4,256,256]{2,1,0:T(8,128)(2,1)}, u32[]{:S(2)}) copy-start(bf16[4,256,256]{2,1,0:T(8,128)(2,1)} %param.13) | copy-start | bytes 1572868
  7.2 12.1 %copy-start.3 = (bf16[1024,256]{1,0:T(8,128)(2,1)S(1)}, bf16[1024,256]{1,0:T(8,128)(2,1)}, u32[]{:S(2)}) copy-start(bf16[1024,256]{1,0:T(8,128)(2,1)} %param.11) | copy-start | bytes 1572868
  7.2 12.1 %copy-start.13 = (s32[1,512]{1,0:T(1,128)S(1)}, s32[1,512]{1,0:T(1,128)}, u32[]{:S(2)}) copy-start(s32[1,512]{1,0:T(1,128)} %param.16) | copy-start | bytes 6148
  9.3 16.2 %copy-start.11 = (s32[1,4,1024]{2,1,0:T(4,128)S(1)}, s32[1,4,1024]{2,1,0:T(4,128)}, u32[]{:S(2)}) copy-start(s32[1,4,1024]{2,1,0:T(4,128)} %param.18) | copy-start | bytes 49156
  9.3 20.4 %copy-start.12 = (s32[1,4,1024]{2,1,0:T(4,128)S(1)}, s32[1,4,1024]{2,1,0:T(4,128)}, u32[]{:S(2)}) copy-start(s32[1,4,1024]{2,1,0:T(4,128)} %param.17) | copy-start | bytes 49156
  12.2 36.6 %all-to-all-start = ((s32[32,1,64]{2,1,0:T(1,128)}), s32[32,1,64]{2,1,0:T(1,128)S(1)}, u32[]{:S(2)}, u32[]{:S(2)}) async-start(s32[32,1,64]{2,1,0:T(1,128)} %sub.22), calls=%async_computation | async-start | bytes 32768 | tf_op jit(solution)/shard_map/all_to_all | solution.py:98
  19.9 7.6 %collective-permute-start = (bf16[256,256]{1,0:T(8,128)(2,1)S(1)}, bf16[256,256]{1,0:T(8,128)(2,1)S(1)}, u32[]{:S(2)}, u32[]{:S(2)}) collective-permute-start(bf16[256,256]{1,0:T(8,128)(2,1)S(1)} %get-tuple-element.17), channel_id=1, source_target_pairs={{0,1},{1,2},{2,3},{3,4},{4,5},{5,6},{6,7},{8,9},{9,10},{10,11},{11... | collective-permute-start | bytes 393224 | tf_op jit(solution)/shard_map/ppermute | solution.py:18
  23.4 6.3 %collective-permute-start.1 = (bf16[256,256]{1,0:T(8,128)(2,1)S(1)}, bf16[256,256]{1,0:T(8,128)(2,1)S(1)}, u32[]{:S(2)}, u32[]{:S(2)}) collective-permute-start(bf16[256,256]{1,0:T(8,128)(2,1)S(1)} %get-tuple-element.18), channel_id=1, source_target_pairs={{1,0},{2,1},{3,2},{4,3},{5,4},{6,5},{7,6},{9,8},{10,9},{11,10},{12... | collective-permute-start | bytes 393224 | tf_op jit(solution)/shard_map/ppermute | solution.py:21
  43.1 0.9 copy-start.7
  44.3 1.0 copy-start.5
  45.3 8.1 %copy-start.8 = (bf16[1024]{0:T(1024)(128)(2,1)S(1)}, bf16[1024]{0:T(1024)(128)(2,1)}, u32[]{:S(2)}) copy-start(bf16[1024]{0:T(1024)(128)(2,1)} %param.15) | copy-start | bytes 6148
  48.8 31.6 %all-to-all-start.1 = ((bf16[32,64,256]{2,1,0:T(8,128)(2,1)}), bf16[32,64,256]{2,1,0:T(8,128)(2,1)}, u32[]{:S(2)}, u32[]{:S(2)}) async-start(bf16[32,64,256]{2,1,0:T(8,128)(2,1)} %bitcast.64), calls=%async_computation.1 | async-start | bytes 2097152 | tf_op jit(solution)/shard_map/all_to_all | solution.py:106
  82.7 1.8 copy-start.10
  84.4 8.5 %copy-start.9 = (f32[1,256]{1,0:T(1,128)}, f32[1,256]{1,0:T(1,128)S(1)}, u32[]{:S(2)}) copy-start(f32[1,256]{1,0:T(1,128)S(1)} %fusion.64) | copy-start | bytes 3076
  88.8 52.1 %all-to-all-start.2 = ((bf16[32,64,256]{2,1,0:T(8,128)(2,1)}), bf16[32,64,256]{2,1,0:T(8,128)(2,1)}, u32[]{:S(2)}, u32[]{:S(2)}) async-start(bf16[32,64,256]{2,1,0:T(8,128)(2,1)} %bitcast.65), calls=%async_computation.2 | async-start | bytes 2097152 | tf_op jit(solution)/shard_map/all_to_all | solution.py:130
  92.6 204.8 %all-reduce.3.cloned.1.call-start = ((), (), s32[]{:S(2)}) async-start(), calls=%async_computation.3 | async-start | bytes 4718592 | tf_op jit(solution)/shard_map/psum | solution.py:157
  140.9 3.4 %copy-start.4 = (bf16[1024,256]{1,0:T(8,128)(2,1)S(1)}, bf16[1024,256]{1,0:T(8,128)(2,1)}, u32[]{:S(2)}) copy-start(bf16[1024,256]{1,0:T(8,128)(2,1)} %param.11) | copy-start | bytes 1572868
  148.6 1.3 copy-start.2
  157.7 2.7 copy-start.1
  165.2 5.6 %collective-permute-start.2 = (bf16[256,256]{1,0:T(8,128)(2,1)S(1)}, bf16[256,256]{1,0:T(8,128)(2,1)S(1)}, u32[]{:S(2)}, u32[]{:S(2)}) collective-permute-start(bf16[256,256]{1,0:T(8,128)(2,1)S(1)} %get-tuple-element.15), channel_id=1, source_target_pairs={{0,1},{1,2},{2,3},{3,4},{4,5},{5,6},{6,7},{8,9},{9,10},{10,11},{11... | collective-permute-start | bytes 393224 | tf_op jit(solution)/shard_map/ppermute | solution.py:18
  168.1 7.3 %collective-permute-start.3 = (bf16[256,256]{1,0:T(8,128)(2,1)S(1)}, bf16[256,256]{1,0:T(8,128)(2,1)S(1)}, u32[]{:S(2)}, u32[]{:S(2)}) collective-permute-start(bf16[256,256]{1,0:T(8,128)(2,1)S(1)} %get-tuple-element.16), channel_id=1, source_target_pairs={{1,0},{2,1},{3,2},{4,3},{5,4},{6,5},{7,6},{9,8},{10,9},{11,10},{12... | collective-permute-start | bytes 393224 | tf_op jit(solution)/shard_map/ppermute | solution.py:21
  297.4 4.2 %copy-start.6 = (f32[256,1024]{1,0:T(8,128)S(1)}, f32[256,1024]{1,0:T(8,128)}, u32[]{:S(2)}) copy-start(f32[256,1024]{1,0:T(8,128)} %get-tuple-element.14) | copy-start | bytes 3145732
Sparse Core Ops, SparseCore 0:
  161.5 135.8 all-reduce.2

commit v2 on v1

--- a/solution.py
+++ b/solution.py
@@ -33,10 +33,8 @@
 
 
 def split_dot(spec, left, right):
-    head = left.astype(BF16)
-    tail = (left - head.astype(F32)).astype(BF16)
-    return jnp.einsum(spec, head, right, preferred_element_type=F32) + jnp.einsum(
-        spec, tail, right, preferred_element_type=F32
+    return jnp.einsum(
+        spec, left, right.astype(F32), precision=lax.Precision.HIGHEST, preferred_element_type=F32
     )
 
 
@@ -122,7 +120,7 @@
     ).astype(BF16)
     head_sum = jnp.einsum("nd,nh->dh", pooled_b, head_grad, preferred_element_type=F32)
     out_sum = jnp.dot(misfit, activated.astype(F32), precision=lax.Precision.HIGHEST)
-    head_totals = lax.psum((head_sum, out_sum), ("group", "dom"))
+    head_totals = lax.psum(jnp.concatenate([head_sum, out_sum[None, :]], 0), ("group", "dom"))
     net_grad = jnp.einsum(
         "nh,dh->nd", head_grad, w_head, preferred_element_type=F32
     ).astype(BF16)
@@ -154,6 +152,7 @@
     grad_feats = (
         local_grad + jnp.einsum("sp,sd->pd", send_hot, received, preferred_element_type=F32)
     ).astype(BF16)
+    self_sum, edge_sum, head_totals = lax.optimization_barrier((self_sum, edge_sum, head_totals))
     tail_totals = lax.psum((self_sum, edge_sum), ("group", "dom"))
     grad_scale = 1.0 / math.sqrt(pin_count * owners)
     return (
@@ -161,8 +160,8 @@
         grad_feats,
         tail_totals[0] * grad_scale,
         tail_totals[1] * grad_scale,
-        head_totals[0] * grad_scale,
-        head_totals[1] * grad_scale,
+        head_totals[:feat_width] * grad_scale,
+        head_totals[feat_width] * grad_scale,
     )
 
 

time: 312 us -> 385 us (1.23)
  waiting for transfers between devices: 153 us -> 269 us
  blocking collectives: 45 us -> 0 us
    psum x0 -> x1, waiting for transfers between devices: none -> 90 us  [on_device(): lax.psum(jnp.concatenate([head_sum, out_sum[None, :]], 0), ('group', 'dom'))]
    psum x1 -> x0, blocking collectives: 45 us -> none  [on_device(): head_totals = lax.psum((head_sum, out_sum), ('group', 'dom'))]
    all_to_all x1, waiting for transfers between devices: 0.01 us -> 26.4 us  [on_device(): lax.all_to_all(returned.reshape(owners, capacity, feat_width), ('group',...]
    ppermute x2, waiting for transfers between devices: 6.72 us -> 2.35 us  [extended(): lax.ppermute(lax.slice_in_dim(block, 0, width, axis=dim), axis, backward)]
  transfers between devices with their start and end apart: 8 -> 9, of which waited for: 5 -> 6; matrix products, arithmetic and copies ran while one was open for 10% -> 13% of each run, Pallas kernels for 0% -> 0%
where the time goes in v2:
time: 385 us; the launch traced here: 382 us
  waiting for transfers between devices  269 us (70%)
  matrix products  54.3 us (14%)
  starting transfers between devices  27.4 us (7%)
  between operations  14.4 us (4%)
  other arithmetic  13.6 us (4%)
  local copies, waits for them, and re-layouts  3.99 us (1%)
    psum x1, waiting for transfers between devices, on_device(): tail_totals = lax.psum((self_sum, edge_sum), ('group', 'dom'))  124 us
    psum x1, waiting for transfers between devices, on_device(): lax.psum(jnp.concatenate([head_sum, out_sum[None, :]], 0), ('group', 'dom'))  90 us
    all_to_all x1, waiting for transfers between devices, on_device(): lax.all_to_all(returned.reshape(owners, capacity, feat_width), ('group',...  26.4 us
    all_to_all x1, waiting for transfers between devices, on_device(): lax.all_to_all(outbound.reshape(owners, capacity, feat_width), ('group',...  25.7 us
    dot_general x1, matrix products, on_device(): jnp.einsum('ter,ted->trd', src_hot, edge_rows, preferred_element_type=F32)  9.33 us
    ppermute x2, starting transfers between devices, extended(): lax.ppermute(lax.slice_in_dim(block, block.shape[dim] - width, None, axis...  8.05 us
  transfers between devices with their start and end apart: 9, of which 6 were waited for; matrix products, arithmetic and copies ran while one was open for 13% of the time, Pallas kernels for 0%

profile of v2, /device:TPU:1, one launch (start us, length us, event | category | flops | bytes accessed | tf_op | source)
XLA Modules:
  0.0 382.4 jit_solution(4948331850442410509)
XLA Ops:
  7.2 0.0 copy-start
  7.2 0.7 add_convert_fusion
  7.9 1.3 fusion.31
  9.2 0.0 copy-start.2
  9.2 0.0 copy-start.14
  9.3 0.7 multiply_add_fusion
  10.0 1.5 fusion.11
  11.5 0.7 sub.16
  12.2 7.1 %all-to-all-start = ((s32[32,1,64]{2,1,0:T(1,128)}), s32[32,1,64]{2,1,0:T(1,128)S(1)}, u32[]{:S(2)}, u32[]{:S(2)}) async-start(s32[32,1,64]{2,1,0:T(1,128)} %sub.16), calls=%async_computation | async-start | bytes 32768 | tf_op jit(solution)/shard_map/all_to_all | solution.py:96
  19.3 0.5 fusion.28
  19.9 3.5 collective-permute-start
  23.4 1.9 collective-permute-start.1
  25.4 1.9 convert_reduce_fusion
  27.3 0.3 fusion.55
  27.6 0.0 collective-permute-done
  27.6 2.1 collective-permute-done.1
  29.7 4.8 %fusion.20 = bf16[4,1024,256]{2,1,0:T(8,128)(2,1)S(1)} fusion(s32[4,1024]{1,0:T(4,128)S(1)} %bitcast.74, bf16[256,256]{1,0:T(8,128)(2,1)S(1)} %collective-permute-done.1, bf16[256,256]{1,0:T(8,128)(2,1)S(1)} %collective-permute-done, bf16[1024,256]{1,0:T(8,128)(2,1)S(1)} %copy-done.2), kind=kOutput, calls=%fused_computation.29 | convolution fusion | flops 3230924800 | bytes 2899968 | tf_op jit(solution)/shard_map/ter,rd->ted/dot_general | solution.py:66
  34.5 0.0 copy-start.1
  34.6 5.8 %fusion.4 = f32[4,1024,256]{2,1,0:T(8,128)S(1)} fusion(bf16[4,1024,256]{2,1,0:T(8,128)(2,1)S(1)} %fusion.20, s32[4,1024]{1,0:T(4,128)S(1)} %bitcast.72), kind=kOutput, calls=%fused_computation.7 | convolution fusion | flops 2151677952 | bytes 6307840 | tf_op jit(solution)/shard_map/tep,ted->tpd/dot_general | solution.py:69
  40.3 2.1 fusion.24
  42.4 0.0 copy-start.7
  42.4 1.0 copy-done.7
  43.4 3.5 fusion.16
  46.9 4.5 %all-to-all-start.1 = ((bf16[32,64,256]{2,1,0:T(8,128)(2,1)}), bf16[32,64,256]{2,1,0:T(8,128)(2,1)}, u32[]{:S(2)}, u32[]{:S(2)}) async-start(bf16[32,64,256]{2,1,0:T(8,128)(2,1)} %bitcast.60), calls=%async_computation.1 | async-start | bytes 2097152 | tf_op jit(solution)/shard_map/all_to_all | solution.py:104
  51.5 0.5 broadcast.42
  52.0 0.7 reduce.3
  52.7 0.1 eq.98
  52.8 25.7 %all-to-all-done.1 = bf16[32,64,256]{2,1,0:T(8,128)(2,1)} async-done(((bf16[32,64,256]{2,1,0:T(8,128)(2,1)}), bf16[32,64,256]{2,1,0:T(8,128)(2,1)}, u32[]{:S(2)}, u32[]{:S(2)}) %all-to-all-start.1) | async-done | bytes 1048608 | tf_op jit(solution)/shard_map/all_to_all | solution.py:104
  78.5 2.3 fusion.29
  80.8 0.0 copy-start.11
  80.8 0.5 multiply_convert_fusion.2
  81.3 0.8 copy-done.4
  82.1 0.2 fusion.56
  82.3 1.2 multiply_convert_fusion.1
  83.5 3.0 convolution_convert_fusion
  86.5 3.8 all-to-all-start.2
  90.3 0.0 all-reduce.4.cloned.1.call-start
  90.3 1.4 fusion.59
  91.7 1.4 fusion.58
  93.1 1.2 pad_maximum_fusion
  94.3 0.0 all-reduce.4.cloned.1.call-update
  94.3 0.0 all-reduce.6.cloned.1.call-start
  94.4 26.4 %all-to-all-done.2 = bf16[32,64,256]{2,1,0:T(8,128)(2,1)} async-done(((bf16[32,64,256]{2,1,0:T(8,128)(2,1)}), bf16[32,64,256]{2,1,0:T(8,128)(2,1)}, u32[]{:S(2)}, u32[]{:S(2)}) %all-to-all-start.2) | async-done | bytes 1048608 | tf_op jit(solution)/shard_map/all_to_all | solution.py:128
  120.7 3.3 fusion.26
  124.0 0.0 copy-start.5
  124.1 3.3 fusion.21
  127.4 0.0 copy-start.3
  127.4 9.3 %fusion = f32[4,1536,256]{2,1,0:T(8,128)} fusion(bf16[4,1024,256]{2,1,0:T(8,128)(2,1)S(1)} %fusion.21, s32[4,1024]{1,0:T(4,128)S(1)} %bitcast.75), kind=kOutput, calls=%fused_computation.1 | convolution fusion | flops 3227516928 | bytes 8404992 | tf_op jit(solution)/shard_map/ter,ted->trd/dot_general | solution.py:143
  136.7 1.0 convolution_bitcast_fusion.2
  137.7 1.9 fusion.57
  139.6 90.0 %all-reduce.4.cloned.1.call-done = f32[257,1024]{1,0:T(8,128)} async-done(((f32[257,1024]{1,0:T(8,128)}), f32[257,1024]{1,0:T(8,128)}) %all-reduce.4.cloned.1.call-update) | async-done | bytes 1052688 | tf_op jit(solution)/shard_map/psum | solution.py:123
  229.7 5.1 %fusion.54 = (bf16[1536,256]{1,0:T(8,128)(2,1)S(1)}, f32[1536,256]{1,0:T(8,128)S(1)}) fusion(f32[4,1536,256]{2,1,0:T(8,128)} %fusion, bf16[4,256,256]{2,1,0:T(8,128)(2,1)S(1)} %copy-done.1), kind=kOutput, calls=%fused_computation.83 | convolution fusion | flops 4832231424 | bytes 9175040 | tf_op jit(solution)/shard_map/trd,tkd->rk/dot_general | solution.py:36
  234.8 4.5 %collective-permute-start.2 = (bf16[256,256]{1,0:T(8,128)(2,1)S(1)}, bf16[256,256]{1,0:T(8,128)(2,1)S(1)}, u32[]{:S(2)}, u32[]{:S(2)}) collective-permute-start(bf16[256,256]{1,0:T(8,128)(2,1)S(1)} %get-tuple-element.20), channel_id=1, source_target_pairs={{0,1},{1,2},{2,3},{3,4},{4,5},{5,6},{6,7},{8,9},{9,10},{10,11},{11... | collective-permute-start | bytes 393224 | tf_op jit(solution)/shard_map/ppermute | solution.py:18
  239.3 1.9 collective-permute-start.3
  241.3 0.3 convolution_add_fusion
  241.6 0.0 all-reduce.6.cloned.1.call-update
  241.6 2.3 slice_multiply_fusion
  244.0 1.4 slice_multiply_fusion.1
  245.3 0.3 collective-permute-done.3
  245.6 1.6 fusion.27
  247.2 124.2 %all-reduce.6.cloned.1.call-done = (f32[256,256]{0,1:T(8,128)}, f32[4,256,256]{2,1,0:T(8,128)}) async-done(((f32[256,256]{0,1:T(8,128)}, f32[4,256,256]{2,1,0:T(8,128)}), (f32[256,256]{0,1:T(8,128)}, f32[4,256,256]{2,1,0:T(8,128)})) %all-reduce.6.cloned.1.call-update) | async-done | bytes 1310736 | tf_op jit(solution)/shard_map/psum | solution.py:156
  371.4 1.0 broadcast_multiply_fusion.1
  372.4 0.8 copy.18
  373.3 2.3 broadcast_multiply_fusion
  (31 shorter events, 0.1 us)
Async XLA Ops:
  7.2 73.6 %copy-start = (bf16[256,1024]{1,0:T(8,128)(2,1)S(1)}, bf16[256,1024]{1,0:T(8,128)(2,1)}, u32[]{:S(2)}) copy-start(bf16[256,1024]{1,0:T(8,128)(2,1)} %param.14) | copy-start | bytes 1572868
  9.2 10.1 %copy-start.2 = (bf16[1024,256]{1,0:T(8,128)(2,1)S(1)}, bf16[1024,256]{1,0:T(8,128)(2,1)}, u32[]{:S(2)}) copy-start(bf16[1024,256]{1,0:T(8,128)(2,1)} %param.11) | copy-start | bytes 1572868
  9.2 10.1 %copy-start.14 = (s32[1,512]{1,0:T(1,128)S(1)}, s32[1,512]{1,0:T(1,128)}, u32[]{:S(2)}) copy-start(s32[1,512]{1,0:T(1,128)} %param.16) | copy-start | bytes 6148
  10.0 15.3 %copy-start.12 = (s32[1,4,1024]{2,1,0:T(4,128)S(1)}, s32[1,4,1024]{2,1,0:T(4,128)}, u32[]{:S(2)}) copy-start(s32[1,4,1024]{2,1,0:T(4,128)} %param.18) | copy-start | bytes 49156
  10.0 17.3 %copy-start.8 = (bf16[256,256]{1,0:T(8,128)(2,1)S(1)}, bf16[256,256]{1,0:T(8,128)(2,1)}, u32[]{:S(2)}) copy-start(bf16[256,256]{1,0:T(8,128)(2,1)} %param.12) | copy-start | bytes 393220
  11.5 18.2 %copy-start.13 = (s32[1,4,1024]{2,1,0:T(4,128)S(1)}, s32[1,4,1024]{2,1,0:T(4,128)}, u32[]{:S(2)}) copy-start(s32[1,4,1024]{2,1,0:T(4,128)} %param.17) | copy-start | bytes 49156
  12.2 34.7 %all-to-all-start = ((s32[32,1,64]{2,1,0:T(1,128)}), s32[32,1,64]{2,1,0:T(1,128)S(1)}, u32[]{:S(2)}, u32[]{:S(2)}) async-start(s32[32,1,64]{2,1,0:T(1,128)} %sub.16), calls=%async_computation | async-start | bytes 32768 | tf_op jit(solution)/shard_map/all_to_all | solution.py:96
  19.9 7.8 %collective-permute-start = (bf16[256,256]{1,0:T(8,128)(2,1)S(1)}, bf16[256,256]{1,0:T(8,128)(2,1)S(1)}, u32[]{:S(2)}, u32[]{:S(2)}) collective-permute-start(bf16[256,256]{1,0:T(8,128)(2,1)S(1)} %get-tuple-element.22), channel_id=1, source_target_pairs={{0,1},{1,2},{2,3},{3,4},{4,5},{5,6},{6,7},{8,9},{9,10},{10,11},{11... | collective-permute-start | bytes 393224 | tf_op jit(solution)/shard_map/ppermute | solution.py:18
  23.4 6.3 %collective-permute-start.1 = (bf16[256,256]{1,0:T(8,128)(2,1)S(1)}, bf16[256,256]{1,0:T(8,128)(2,1)S(1)}, u32[]{:S(2)}, u32[]{:S(2)}) collective-permute-start(bf16[256,256]{1,0:T(8,128)(2,1)S(1)} %get-tuple-element.23), channel_id=1, source_target_pairs={{1,0},{2,1},{3,2},{4,3},{5,4},{6,5},{7,6},{9,8},{10,9},{11,10},{12... | collective-permute-start | bytes 393224 | tf_op jit(solution)/shard_map/ppermute | solution.py:21
  34.5 5.8 %copy-start.1 = (bf16[4,256,256]{2,1,0:T(8,128)(2,1)S(1)}, bf16[4,256,256]{2,1,0:T(8,128)(2,1)}, u32[]{:S(2)}) copy-start(bf16[4,256,256]{2,1,0:T(8,128)(2,1)} %param.13) | copy-start | bytes 1572868
  42.4 1.0 copy-start.7
  46.9 4.6 %copy-start.9 = (bf16[1024]{0:T(1024)(128)(2,1)S(1)}, bf16[1024]{0:T(1024)(128)(2,1)}, u32[]{:S(2)}) copy-start(bf16[1024]{0:T(1024)(128)(2,1)} %param.15) | copy-start | bytes 6148
  46.9 31.6 %all-to-all-start.1 = ((bf16[32,64,256]{2,1,0:T(8,128)(2,1)}), bf16[32,64,256]{2,1,0:T(8,128)(2,1)}, u32[]{:S(2)}, u32[]{:S(2)}) async-start(bf16[32,64,256]{2,1,0:T(8,128)(2,1)} %bitcast.60), calls=%async_computation.1 | async-start | bytes 2097152 | tf_op jit(solution)/shard_map/all_to_all | solution.py:104
  80.8 1.5 copy-start.11
  81.3 0.8 copy-start.4
  82.3 4.2 %copy-start.10 = (f32[1,256]{1,0:T(1,128)}, f32[1,256]{1,0:T(1,128)S(1)}, u32[]{:S(2)}) copy-start(f32[1,256]{1,0:T(1,128)S(1)} %fusion.56) | copy-start | bytes 3076
  86.5 34.2 %all-to-all-start.2 = ((bf16[32,64,256]{2,1,0:T(8,128)(2,1)}), bf16[32,64,256]{2,1,0:T(8,128)(2,1)}, u32[]{:S(2)}, u32[]{:S(2)}) async-start(bf16[32,64,256]{2,1,0:T(8,128)(2,1)} %bitcast.59), calls=%async_computation.2 | async-start | bytes 2097152 | tf_op jit(solution)/shard_map/all_to_all | solution.py:128
  90.3 139.4 %all-reduce.4.cloned.1.call-start = ((), (), s32[]{:S(2)}) async-start(), calls=%async_computation.3 | async-start | bytes 2162688 | tf_op jit(solution)/shard_map/psum | solution.py:123
  94.3 277.1 %all-reduce.6.cloned.1.call-start = ((), (), s32[]{:S(2)}) async-start(), calls=%async_computation.4 | async-start | bytes 2621440 | tf_op jit(solution)/shard_map/psum | solution.py:156
  124.0 12.7 %copy-start.5 = (bf16[1024,256]{1,0:T(8,128)(2,1)}, bf16[1024,256]{1,0:T(8,128)(2,1)S(1)}, u32[]{:S(2)}) copy-start(bf16[1024,256]{1,0:T(8,128)(2,1)S(1)} %fusion.26) | copy-start | bytes 1572868
  127.4 9.4 %copy-start.3 = (bf16[1024,256]{1,0:T(8,128)(2,1)S(1)}, bf16[1024,256]{1,0:T(8,128)(2,1)}, u32[]{:S(2)}) copy-start(bf16[1024,256]{1,0:T(8,128)(2,1)} %param.11) | copy-start | bytes 1572868
  139.6 101.6 %copy-start.6 = (bf16[1024,256]{1,0:T(8,128)(2,1)S(1)}, bf16[1024,256]{1,0:T(8,128)(2,1)}, u32[]{:S(2)}) copy-start(bf16[1024,256]{1,0:T(8,128)(2,1)} %copy-done.5) | copy-start | bytes 1572868
  234.8 10.5 %collective-permute-start.2 = (bf16[256,256]{1,0:T(8,128)(2,1)S(1)}, bf16[256,256]{1,0:T(8,128)(2,1)S(1)}, u32[]{:S(2)}, u32[]{:S(2)}) collective-permute-start(bf16[256,256]{1,0:T(8,128)(2,1)S(1)} %get-tuple-element.20), channel_id=1, source_target_pairs={{0,1},{1,2},{2,3},{3,4},{4,5},{5,6},{6,7},{8,9},{9,10},{10,11},{11... | collective-permute-start | bytes 393224 | tf_op jit(solution)/shard_map/ppermute | solution.py:18
  239.3 6.3 %collective-permute-start.3 = (bf16[256,256]{1,0:T(8,128)(2,1)S(1)}, bf16[256,256]{1,0:T(8,128)(2,1)S(1)}, u32[]{:S(2)}, u32[]{:S(2)}) collective-permute-start(bf16[256,256]{1,0:T(8,128)(2,1)S(1)} %get-tuple-element.21), channel_id=1, source_target_pairs={{1,0},{2,1},{3,2},{4,3},{5,4},{6,5},{7,6},{9,8},{10,9},{11,10},{12... | collective-permute-start | bytes 393224 | tf_op jit(solution)/shard_map/ppermute | solution.py:21
Sparse Core Ops, SparseCore 0:
  96.6 133.0 all-reduce.3
  241.7 129.6 all-reduce.5
